TPU v7x, 512 devices: a whole 4x4x16 slice. The times are simulated.
512 devices in a mesh: section: 32 (over z_hi, y, core), tp: 16 (over z_lo, x).
Axes of the slice: x: 4, y: 4, z: 16 (z_hi: 4, z_lo: 4; z = z_hi * 4 + z_lo), core: 2. Of those that a mesh axis runs over, the one named last changes fastest.
Arguments:
- grad_in: bfloat16 [32, 160, 8192], P('section', None, 'tp'), may hold values from -6 to 6
- out_proj: bfloat16 [32, 4096, 8192], P('section', 'tp'), may hold values from -0.09375 to 0.09375
- value_proj: bfloat16 [32, 8192, 512], P('section', 'tp'), may hold values from -0.0625 to 0.0625
- head_delta: bfloat16 [32, 160, 4096], P('section', None, 'tp'), may hold values from -6 to 6
- pattern: bfloat16 [32, 32, 160, 160], P('section', 'tp'), may hold values from 0 to 0.25
- positions: int32 [160], replicated, may hold values from -1 to 31, as said below
- node_map: int32 [32, 32], P('section'), may hold values from 0 to 31, each once within a row
Outputs:
- residual_grad: bfloat16 [32, 160, 8192], P('section', None, 'tp')
- edge_scores: float32 [32, 32, 32], P('section')
Inputs may be any that keep to these rules, and one draw needn't show every extreme that they name: positions[t] = (t mod 32) - p, or -1 where that is negative, with one left padding p of 0 to 15 for each block of 32 tokens; the first block is unpadded. `node_map`: each row names every node once.
All inputs are finite; a program needn't handle non-finite values.
Results may differ from a plain program's by a relative error of at most 0.0095.
Values may be sent and summed in bfloat16 or wider, within the bound.
No kernel may reach another device: no remote copies, remote signals or barrier semaphores. Data moves between devices by JAX's collectives and lax.ppermute only.
A program may use at most 128 MiB of HBM per device.

v0:
```python
import jax
import jax.numpy as jnp
from jax import lax
from jax.sharding import PartitionSpec as P

HEADS = 32
HEAD_DIM = 128
KV = 4
PROMPT = 32
GROUP = 8


def on_device(grad_in, out_proj, value_proj, head_delta, pattern, positions, node_map):
    tokens = grad_in.shape[1]
    local_width = grad_in.shape[2]
    own_rows = out_proj.shape[1]
    own_heads = own_rows // HEAD_DIM
    width = out_proj.shape[2]
    tp_count = lax.axis_size("tp")
    section_count = lax.axis_size("section")
    weights = out_proj[0]
    blocks = weights.reshape(own_rows, tp_count, width // tp_count).transpose(1, 0, 2)
    column_blocks = lax.all_to_all(blocks, "tp", 0, 0, tiled=True)
    all_delta_cols = lax.all_gather(head_delta[0], "tp", axis=1, tiled=True)
    token_ids = jnp.arange(tokens)
    block_ids = token_ids // PROMPT
    allowed = (
        (block_ids[:, None] == block_ids[None, :])
        & (positions[None, :] >= 0)
        & (positions[None, :] <= positions[:, None])
    )
    visible = allowed.astype(jnp.bfloat16)
    grad_rows = lax.all_gather(grad_in[0], "tp", axis=1, tiled=True)
    head_grad = lax.dot_general(
        grad_rows, weights, (((1,), (1,)), ((), ())), preferred_element_type=jnp.float32
    ).astype(jnp.bfloat16)
    masked = pattern[0] * visible[None]
    value_grad = jnp.einsum(
        "hts,thc->shc",
        masked,
        head_grad.reshape(tokens, own_heads, HEAD_DIM),
        preferred_element_type=jnp.float32,
    ).astype(jnp.bfloat16)
    pair_sum = value_grad.astype(jnp.float32).sum(axis=1)
    group_of = lax.axis_index("tp") * own_heads // GROUP
    slots = jnp.zeros((tokens, KV, HEAD_DIM), jnp.float32)
    slots = lax.dynamic_update_slice(slots, pair_sum[:, None, :], (0, group_of, 0))
    summed = lax.psum(slots, "tp")
    group_grad = summed.reshape(tokens, KV * HEAD_DIM).astype(jnp.bfloat16)
    increment = lax.dot_general(
        group_grad, value_proj[0], (((1,), (1,)), ((), ())), preferred_element_type=jnp.float32
    )
    residual_grad = (grad_in[0].astype(jnp.float32) + increment).astype(jnp.bfloat16)
    target_row = increment.astype(jnp.bfloat16)
    target_rows = lax.all_gather(target_row[None], "section", axis=0, tiled=True)
    delta = jnp.einsum(
        "thc,hcd->htd",
        all_delta_cols.reshape(tokens, HEADS, HEAD_DIM),
        column_blocks.reshape(HEADS, HEAD_DIM, local_width),
        preferred_element_type=jnp.float32,
    ).astype(jnp.bfloat16)
    partial_scores = lax.dot_general(
        delta.reshape(HEADS, tokens * local_width),
        target_rows.reshape(section_count, tokens * local_width),
        (((1,), (1,)), ((), ())),
        preferred_element_type=jnp.float32,
    )
    totals = lax.psum(partial_scores, "tp")
    later = jnp.arange(section_count) > lax.axis_index("section")
    raw_scores = jnp.where(later[None, :], totals / tokens, jnp.zeros_like(totals))
    onehot = (node_map[0][:, None] == jnp.arange(HEADS)[None, :]).astype(jnp.float32)
    edge_scores = jnp.dot(onehot.T, raw_scores, precision=lax.Precision.HIGHEST)
    return (residual_grad[None], edge_scores[None])


def solution(mesh):
    placed = (
        P("section", None, "tp"),
        P("section", "tp", None),
        P("section", "tp", None),
        P("section", None, "tp"),
        P("section", "tp", None, None),
        P(),
        P("section", None),
    )
    return jax.shard_map(
        on_device,
        mesh=mesh,
        in_specs=placed,
        out_specs=(P("section", None, "tp"), P("section", None, None)),
        check_vma=False,
    )
```

profile of v0, /device:TPU:8, one launch (start us, length us, event | category | flops | bytes accessed | tf_op | source)
XLA Modules:
  0.0 441.4 jit_solution(2010720892174601740)
XLA Ops:
  7.2 0.0 copy-start
  7.2 0.0 all-gather.7.cloned.1.call-start
  7.2 0.7 all-gather.7.cloned.1.call-update
  7.9 6.4 %copy.21 = bf16[1,256,8192]{1,2,0:T(8,128)(2,1)} copy(bf16[1,256,8192]{2,1,0:T(8,128)(2,1)} %param.8) | data formatting | bytes 8388608 | tf_op args[1]
  14.3 8.6 %all-to-all-start = ((bf16[16,256,512]{1,2,0:T(8,128)(2,1)}), bf16[16,256,512]{1,2,0:T(8,128)(2,1)}, u32[]{:S(2)}, u32[]{:S(2)}) async-start(bf16[16,256,512]{1,2,0:T(8,128)(2,1)} %bitcast.55), calls=%async_computation | async-start | bytes 8388608 | tf_op jit(solution)/shard_map/all_to_all | solution.py:23
  23.0 0.0 all-gather.9.cloned.1.call-start
  23.0 0.7 all-gather.9.cloned.1.call-update
  23.7 0.0 all-gather.11.cloned.1.call-start
  23.8 0.1 and_convert_fusion
  24.0 125.0 %all-gather.7.cloned.1.call-done = bf16[1,160,8192]{2,1,0:T(8,128)(2,1)} async-done(((bf16[1,160,512]{2,1,0:T(8,128)(2,1)}), bf16[1,160,8192]{2,1,0:T(8,128)(2,1)}) %all-gather.7.cloned.1.call-update) | async-done | bytes 2621456 | tf_op jit(solution)/shard_map/all_gather | solution.py:33
  149.0 4.5 %fusion.14 = bf16[20,2,8,128]{3,2,1,0:T(8,128)(2,1)S(1)} fusion(bf16[1,256,8192]{2,1,0:T(8,128)(2,1)} %param.8, bf16[1,160,8192]{2,1,0:T(8,128)(2,1)} %all-gather.7.cloned.1.call-done), kind=kOutput, calls=%fused_computation.12 | convolution fusion | flops 671129600 | bytes 6897664 | tf_op jit(solution)/shard_map/dot_general | solution.py:34
  153.5 0.2 fusion.13
  153.8 2.7 dynamic_update_slice.3
  156.6 78.9 %all-reduce.1 = bf16[160,4,128]{2,1,0:T(4,128)(2,1)S(1)} all-reduce(f32[160,4,128]{2,1,0:T(4,128)S(1)} %dynamic_update_slice.3), channel_id=1, replica_groups=mesh['section'=32,'tp'=16] {'tp'}, use_global_device_ids=true, to_apply=%region_1.2 | all-reduce | flops 81920 | bytes 491520 | tf_op jit(solution)/shard_map/psum | solution.py:48
  235.5 1.0 fusion.41
  236.6 0.0 all-gather.11.cloned.1.call-update
  236.6 0.0 all-gather.9.cloned.1.call-done
  236.6 1.6 copy.29
  238.2 6.4 %copy.22 = bf16[16,256,512]{2,1,0:T(8,128)(2,1)} copy(bf16[16,256,512]{1,2,0:T(8,128)(2,1)} %all-to-all-done) | data formatting | bytes 8388608 | tf_op jit(solution)/shard_map/all_to_all | solution.py:23
  244.6 6.0 %convolution_convert_fusion = bf16[32,160,512]{2,1,0:T(8,128)(2,1)} fusion(bf16[32,128,512]{2,1,0:T(8,128)(2,1)} %bitcast.56, bf16[160,32,128]{2,1,0:T(8,128)(2,1)S(1)} %bitcast.57), kind=kOutput, calls=%fused_computation.5 | convolution fusion | flops 673710080 | bytes 10747904 | tf_op jit(solution)/shard_map/thc,hcd->htd/dot_general | solution.py:56
  250.7 92.8 %all-gather.11.cloned.1.call-done = bf16[5120,512]{1,0:T(8,128)(2,1)} async-done(((bf16[160,512]{1,0:T(8,128)(2,1)}), bf16[5120,512]{1,0:T(8,128)(2,1)}) %all-gather.11.cloned.1.call-update) | async-done | bytes 5242896 | tf_op jit(solution)/shard_map/all_gather | solution.py:55
  343.5 15.0 %fusion.19 = f32[32,32]{1,0:T(8,128)S(1)} fusion(bf16[32,160,512]{2,1,0:T(8,128)(2,1)} %bitcast.61, bf16[32,160,512]{2,1,0:T(8,128)(2,1)} %convolution_convert_fusion), kind=kOutput, calls=%fused_computation.13 | convolution fusion | flops 167772160 | bytes 10489856 | tf_op jit(solution)/shard_map/dot_general | solution.py:62
  358.5 75.6 %psum.15 = f32[32,32]{1,0:T(8,128)S(1)} all-reduce(f32[32,32]{1,0:T(8,128)S(1)} %fusion.19), channel_id=1, replica_groups=mesh['section'=32,'tp'=16] {'tp'}, use_global_device_ids=true, to_apply=%region_2.3 | all-reduce | flops 1024 | bytes 8192 | tf_op jit(solution)/shard_map/psum | solution.py:68
  434.0 0.9 convolution_bitcast_fusion
  (14 shorter events, 0.1 us)
Async XLA Ops:
  7.2 228.3 %copy-start = (bf16[1,512,512]{2,1,0:T(8,128)(2,1)S(1)}, bf16[1,512,512]{2,1,0:T(8,128)(2,1)}, u32[]{:S(2)}) copy-start(bf16[1,512,512]{2,1,0:T(8,128)(2,1)} %param.9) | copy-start | bytes 1572868
  7.2 141.8 %all-gather.7.cloned.1.call-start = ((), (), s32[]{:S(2)}) async-start(), calls=%async_computation.1 | async-start | bytes 2785280 | tf_op jit(solution)/shard_map/all_gather | solution.py:33
  14.3 9.5 %copy-start.3 = (s32[160]{0:T(256)S(1)}, s32[160]{0:T(256)}, u32[]{:S(2)}) copy-start(s32[160]{0:T(256)} %param.12) | copy-start | bytes 1924
  14.3 223.9 %all-to-all-start = ((bf16[16,256,512]{1,2,0:T(8,128)(2,1)}), bf16[16,256,512]{1,2,0:T(8,128)(2,1)}, u32[]{:S(2)}, u32[]{:S(2)}) async-start(bf16[16,256,512]{1,2,0:T(8,128)(2,1)} %bitcast.55), calls=%async_computation | async-start | bytes 8388608 | tf_op jit(solution)/shard_map/all_to_all | solution.py:23
  23.0 213.6 %all-gather.9.cloned.1.call-start = ((), (), s32[]{:S(2)}) async-start(), calls=%async_computation.2 | async-start | bytes 1392640 | tf_op jit(solution)/shard_map/all_gather | solution.py:24
  23.7 319.7 %all-gather.11.cloned.1.call-start = ((), (), s32[]{:S(2)}) async-start(), calls=%async_computation.3 | async-start | bytes 5406720 | tf_op jit(solution)/shard_map/all_gather | solution.py:55
  24.0 129.5 %copy-start.2 = (bf16[1,2,160,160]{3,2,1,0:T(8,128)(2,1)S(1)}, bf16[1,2,160,160]{3,2,1,0:T(8,128)(2,1)}, u32[]{:S(2)}) copy-start(bf16[1,2,160,160]{3,2,1,0:T(8,128)(2,1)} %param.11) | copy-start | bytes 307204
  24.0 211.5 %copy-start.1 = (bf16[1,160,512]{2,1,0:T(8,128)(2,1)S(1)}, bf16[1,160,512]{2,1,0:T(8,128)(2,1)}, u32[]{:S(2)}) copy-start(bf16[1,160,512]{2,1,0:T(8,128)(2,1)} %param.7) | copy-start | bytes 491524
  343.5 90.5 %copy-start.4 = (s32[1,32]{1,0:T(1,128)S(1)}, s32[1,32]{1,0:T(1,128)}, u32[]{:S(2)}) copy-start(s32[1,32]{1,0:T(1,128)} %param.13) | copy-start | bytes 388
Sparse Core Ops, SparseCore 0:
  10.1 138.8 all-gather.6
  151.0 73.8 all-gather.8
  236.7 106.7 all-gather.10
where the time goes:
time: 442 us; the launch traced here: 441 us
  waiting for transfers between devices  219 us (50%)
  blocking collectives  154 us (35%)
  matrix products  27.7 us (6%)
  local copies, waits for them, and re-layouts  17.2 us (4%)
  between operations  13.9 us (3%)
  starting transfers between devices  8.77 us (2%)
    all_gather x1, waiting for transfers between devices, on_device(): grad_rows = lax.all_gather(grad_in[0], 'tp', axis=1, tiled=True)  125 us
    all_gather x1, waiting for transfers between devices, on_device(): lax.all_gather(target_row[None], 'section', axis=0, tiled=True)  92.8 us
    psum x1, blocking collectives, on_device(): summed = lax.psum(slots, 'tp')  78.9 us
    psum x1, blocking collectives, on_device(): totals = lax.psum(partial_scores, 'tp')  75.6 us
    dot_general x1, matrix products, on_device(): lax.dot_general(delta.reshape(HEADS, tokens * local_width), target_rows.r...  15 us
  transfers between devices with their start and end apart: 4, of which 2 were waited for; matrix products, arithmetic and copies ran while one was open for 7% of the time, Pallas kernels for 0%

commit v1 on v0

--- a/solution.py
+++ b/solution.py
@@ -1,13 +1,22 @@
+import functools
 import jax
 import jax.numpy as jnp
 from jax import lax
 from jax.sharding import PartitionSpec as P
+from jax.lax import all_gather
 
 HEADS = 32
 HEAD_DIM = 128
 KV = 4
 PROMPT = 32
 GROUP = 8
+
+
+def make_the_floor(body, link_axis):
+    return jnp.sum(all_gather(body, link_axis), 0)
+
+
+expand_the_threads = functools.partial(make_the_floor, link_axis="tp")
 
 
 def on_device(grad_in, out_proj, value_proj, head_delta, pattern, positions, node_map):
@@ -45,7 +54,7 @@
     group_of = lax.axis_index("tp") * own_heads // GROUP
     slots = jnp.zeros((tokens, KV, HEAD_DIM), jnp.float32)
     slots = lax.dynamic_update_slice(slots, pair_sum[:, None, :], (0, group_of, 0))
-    summed = lax.psum(slots, "tp")
+    summed = expand_the_threads(slots)
     group_grad = summed.reshape(tokens, KV * HEAD_DIM).astype(jnp.bfloat16)
     increment = lax.dot_general(
         group_grad, value_proj[0], (((1,), (1,)), ((), ())), preferred_element_type=jnp.float32

time: 442 us -> 549 us (1.24)
  waiting for transfers between devices: 219 us -> 405 us
  blocking collectives: 154 us -> 75.6 us
    all_gather x0 -> x1, waiting for transfers between devices: none -> 121 us  [make_the_floor(): return jnp.sum(all_gather(body, link_axis), 0)]
    all_gather x1, waiting for transfers between devices: 0.02 us -> 90.8 us  [on_device(): all_delta_cols = lax.all_gather(head_delta[0], 'tp', axis=1, tiled=True)]
    psum x1 -> x0, blocking collectives: 78.9 us -> none  [on_device(): summed = lax.psum(slots, 'tp')]
    all_gather x1, waiting for transfers between devices: 125 us -> 95.2 us  [on_device(): grad_rows = lax.all_gather(grad_in[0], 'tp', axis=1, tiled=True)]
  transfers between devices with their start and end apart: 4 -> 5, of which waited for: 2 -> 4; matrix products, arithmetic and copies ran while one was open for 7% -> 5% of each run, Pallas kernels for 0% -> 0%
where the time goes in v1:
time: 549 us; the launch traced here: 548 us
  waiting for transfers between devices  405 us (74%)
  blocking collectives  75.6 us (14%)
  matrix products  27.7 us (5%)
  local copies, waits for them, and re-layouts  15.2 us (3%)
  between operations  13.9 us (3%)
  starting transfers between devices  6.5 us (1%)
    all_gather x1, waiting for transfers between devices, make_the_floor(): return jnp.sum(all_gather(body, link_axis), 0)  121 us
    all_gather x1, waiting for transfers between devices, on_device(): lax.all_gather(target_row[None], 'section', axis=0, tiled=True)  96.5 us
    all_gather x1, waiting for transfers between devices, on_device(): grad_rows = lax.all_gather(grad_in[0], 'tp', axis=1, tiled=True)  95.2 us
    all_gather x1, waiting for transfers between devices, on_device(): all_delta_cols = lax.all_gather(head_delta[0], 'tp', axis=1, tiled=True)  90.8 us
    psum x1, blocking collectives, on_device(): totals = lax.psum(partial_scores, 'tp')  75.6 us
    dot_general x1, matrix products, on_device(): lax.dot_general(delta.reshape(HEADS, tokens * local_width), target_rows.r...  15 us
  transfers between devices with their start and end apart: 5, of which 4 were waited for; matrix products, arithmetic and copies ran while one was open for 5% of the time, Pallas kernels for 0%

profile of v1, /device:TPU:8, one launch (start us, length us, event | category | flops | bytes accessed | tf_op | source)
XLA Modules:
  0.0 548.5 jit_solution(14516808069639608405)
XLA Ops:
  7.2 0.7 all-gather.10.cloned.1.call-update
  7.9 0.0 all-gather.8.cloned.1.call-start
  8.0 0.7 broadcast_compare_fusion
  8.7 0.9 and_convert_fusion
  9.6 95.2 %all-gather.10.cloned.1.call-done = bf16[1,160,8192]{2,1,0:T(8,128)(2,1)} async-done(((bf16[1,160,512]{2,1,0:T(8,128)(2,1)}), bf16[1,160,8192]{2,1,0:T(8,128)(2,1)}) %all-gather.10.cloned.1.call-update) | async-done | bytes 2621456 | tf_op jit(solution)/shard_map/all_gather | solution.py:42
  104.7 4.5 fusion.14
  109.3 0.2 fusion.13
  109.6 0.7 copy-done.1
  110.3 6.4 %copy.43 = bf16[1,256,8192]{1,2,0:T(8,128)(2,1)} copy(bf16[1,256,8192]{2,1,0:T(8,128)(2,1)} %param.8) | data formatting | bytes 8388608 | tf_op args[1]
  116.8 6.3 %all-to-all-start = ((bf16[16,256,512]{1,2,0:T(8,128)(2,1)}), bf16[16,256,512]{1,2,0:T(8,128)(2,1)}, u32[]{:S(2)}, u32[]{:S(2)}) async-start(bf16[16,256,512]{1,2,0:T(8,128)(2,1)} %bitcast.61), calls=%async_computation | async-start | bytes 8388608 | tf_op jit(solution)/shard_map/all_to_all | solution.py:32
  123.1 0.0 all-gather.12.cloned.1.call-start
  123.2 0.7 all-gather.12.cloned.1.call-update
  123.9 0.0 all-gather.14.cloned.1.call-start
  123.9 121.4 %all-gather.8.cloned.1.call-done = f32[16,160,4,128]{3,1,2,0:T(8,128)} async-done(((f32[1,160,4,128]{3,1,2,0:T(8,128)}), f32[16,160,4,128]{3,1,2,0:T(8,128)}) %all-gather.8.cloned.1.call-update) | async-done | bytes 5242896 | tf_op jit(solution)/shard_map/all_gather | solution.py:16
  245.3 2.8 reduce_sum.22
  248.1 1.0 fusion.41
  249.2 90.8 %all-gather.12.cloned.1.call-done = bf16[1,160,4096]{2,1,0:T(8,128)(2,1)} async-done(((bf16[1,160,256]{2,1,0:T(8,128)(2,1)}), bf16[1,160,4096]{2,1,0:T(8,128)(2,1)}) %all-gather.12.cloned.1.call-update) | async-done | bytes 1310736 | tf_op jit(solution)/shard_map/all_gather | solution.py:33
  340.0 1.6 copy.51
  341.6 6.4 %copy.44 = bf16[16,256,512]{2,1,0:T(8,128)(2,1)} copy(bf16[16,256,512]{1,2,0:T(8,128)(2,1)} %all-to-all-done) | data formatting | bytes 8388608 | tf_op jit(solution)/shard_map/all_to_all | solution.py:32
  348.0 6.1 %convolution_convert_fusion = bf16[32,160,512]{2,1,0:T(8,128)(2,1)} fusion(bf16[32,128,512]{2,1,0:T(8,128)(2,1)} %bitcast.62, bf16[160,32,128]{2,1,0:T(8,128)(2,1)S(1)} %bitcast.63), kind=kOutput, calls=%fused_computation.5 | convolution fusion | flops 673710080 | bytes 10747904 | tf_op jit(solution)/shard_map/thc,hcd->htd/dot_general | solution.py:65
  354.1 96.5 %all-gather.14.cloned.1.call-done = bf16[5120,512]{1,0:T(8,128)(2,1)} async-done(((bf16[160,512]{1,0:T(8,128)(2,1)}), bf16[5120,512]{1,0:T(8,128)(2,1)}) %all-gather.14.cloned.1.call-update) | async-done | bytes 5242896 | tf_op jit(solution)/shard_map/all_gather | solution.py:64
  450.6 15.0 %fusion.19 = f32[32,32]{1,0:T(8,128)S(1)} fusion(bf16[32,160,512]{2,1,0:T(8,128)(2,1)} %bitcast.65, bf16[32,160,512]{2,1,0:T(8,128)(2,1)} %convolution_convert_fusion), kind=kOutput, calls=%fused_computation.13 | convolution fusion | flops 167772160 | bytes 10489856 | tf_op jit(solution)/shard_map/dot_general | solution.py:71
  465.5 75.6 %psum.7 = f32[32,32]{1,0:T(8,128)S(1)} all-reduce(f32[32,32]{1,0:T(8,128)S(1)} %fusion.19), channel_id=1, replica_groups=mesh['section'=32,'tp'=16] {'tp'}, use_global_device_ids=true, to_apply=%region_2.3 | all-reduce | flops 1024 | bytes 8192 | tf_op jit(solution)/shard_map/psum | solution.py:77
  541.1 0.9 convolution_bitcast_fusion
  (17 shorter events, 0.1 us)
Async XLA Ops:
  7.2 240.9 %copy-start = (bf16[1,512,512]{2,1,0:T(8,128)(2,1)S(1)}, bf16[1,512,512]{2,1,0:T(8,128)(2,1)}, u32[]{:S(2)}) copy-start(bf16[1,512,512]{2,1,0:T(8,128)(2,1)} %param.9) | copy-start | bytes 1572868
  7.2 97.6 %all-gather.10.cloned.1.call-start = ((), (), s32[]{:S(2)}) async-start(), calls=%async_computation.2 | async-start | bytes 2785280 | tf_op jit(solution)/shard_map/all_gather | solution.py:42
  7.9 237.3 %all-gather.8.cloned.1.call-start = ((), (), s32[]{:S(2)}) async-start(), calls=%async_computation.1 | async-start | bytes 5570560 | tf_op jit(solution)/shard_map/all_gather | solution.py:16
  9.6 99.7 %copy-start.3 = (bf16[1,2,160,160]{3,2,1,0:T(8,128)(2,1)S(1)}, bf16[1,2,160,160]{3,2,1,0:T(8,128)(2,1)}, u32[]{:S(2)}) copy-start(bf16[1,2,160,160]{3,2,1,0:T(8,128)(2,1)} %param.11) | copy-start | bytes 307204
  109.6 0.7 copy-start.1
  116.8 224.8 %all-to-all-start = ((bf16[16,256,512]{1,2,0:T(8,128)(2,1)}), bf16[16,256,512]{1,2,0:T(8,128)(2,1)}, u32[]{:S(2)}, u32[]{:S(2)}) async-start(bf16[16,256,512]{1,2,0:T(8,128)(2,1)} %bitcast.61), calls=%async_computation | async-start | bytes 8388608 | tf_op jit(solution)/shard_map/all_to_all | solution.py:32
  123.1 125.0 %copy-start.2 = (bf16[1,160,512]{2,1,0:T(8,128)(2,1)S(1)}, bf16[1,160,512]{2,1,0:T(8,128)(2,1)}, u32[]{:S(2)}) copy-start(bf16[1,160,512]{2,1,0:T(8,128)(2,1)} %param.7) | copy-start | bytes 491524
  123.1 216.9 %all-gather.12.cloned.1.call-start = ((), (), s32[]{:S(2)}) async-start(), calls=%async_computation.3 | async-start | bytes 1392640 | tf_op jit(solution)/shard_map/all_gather | solution.py:33
  123.9 326.7 %all-gather.14.cloned.1.call-start = ((), (), s32[]{:S(2)}) async-start(), calls=%async_computation.4 | async-start | bytes 5406720 | tf_op jit(solution)/shard_map/all_gather | solution.py:64
  450.6 90.5 %copy-start.4 = (s32[1,32]{1,0:T(1,128)S(1)}, s32[1,32]{1,0:T(1,128)}, u32[]{:S(2)}) copy-start(s32[1,32]{1,0:T(1,128)} %param.13) | copy-start | bytes 388
Sparse Core Ops, SparseCore 0:
  10.1 94.5 all-gather.9
  110.5 134.7 all-gather.7
  247.3 92.6 all-gather.11
  343.0 107.5 all-gather.13

commit v2 on v0

--- a/solution.py
+++ b/solution.py
@@ -52,7 +52,16 @@
     )
     residual_grad = (grad_in[0].astype(jnp.float32) + increment).astype(jnp.bfloat16)
     target_row = increment.astype(jnp.bfloat16)
-    target_rows = lax.all_gather(target_row[None], "section", axis=0, tiled=True)
+    original = target_row[None]
+    target_rows = jnp.concatenate(
+        lax.all_to_all(
+            jnp.stack([original] * lax.axis_size("section")),
+            concat_axis=0,
+            split_axis=0,
+            axis_name="section",
+        ),
+        0,
+    )
     delta = jnp.einsum(
         "thc,hcd->htd",
         all_delta_cols.reshape(tokens, HEADS, HEAD_DIM),

time: 442 us -> 597 us (1.35)
  the two profiles are of different devices: /device:TPU:8 before, /device:TPU:128 now
where the time goes in v2:
time: 597 us; the launch traced here: 596 us
  waiting for transfers between devices  346 us (58%)
  blocking collectives  175 us (29%)
  local copies, waits for them, and re-layouts  26.7 us (4%)
  starting transfers between devices  21.9 us (4%)
  between operations  14.2 us (2%)
  matrix products  11.8 us (2%)
    all_gather x1, waiting for transfers between devices, on_device(): all_delta_cols = lax.all_gather(head_delta[0], 'tp', axis=1, tiled=True)  219 us
    all_gather x1, waiting for transfers between devices, on_device(): grad_rows = lax.all_gather(grad_in[0], 'tp', axis=1, tiled=True)  126 us
    psum x1, blocking collectives, on_device(): totals = lax.psum(partial_scores, 'tp')  97.4 us
    psum x1, blocking collectives, on_device(): summed = lax.psum(slots, 'tp')  77.9 us
    unnamed x16, local copies, waits for them, and re-layouts  16.7 us
    all_to_all x1, starting transfers between devices, on_device(): lax.all_to_all(jnp.stack([original] * lax.axis_size('section')), concat_a...  13 us
  transfers between devices with their start and end apart: 4, of which 2 were waited for; matrix products, arithmetic and copies ran while one was open for 3% of the time, Pallas kernels for 0%

profile of v2, /device:TPU:128, one launch (start us, length us, event | category | flops | bytes accessed | tf_op | source)
XLA Modules:
  0.0 596.4 jit_solution(16338059644333020521)
XLA Ops:
  7.2 4.1 copy.20
  11.3 4.3 copy.36
  15.6 8.6 %all-to-all-start = ((bf16[16,256,512]{2,1,0:T(8,128)(2,1)}), bf16[16,256,512]{2,1,0:T(8,128)(2,1)}, u32[]{:S(2)}, u32[]{:S(2)}) async-start(bf16[16,256,512]{2,1,0:T(8,128)(2,1)} %bitcast.65), calls=%async_computation | async-start | bytes 8388608 | tf_op jit(solution)/shard_map/all_to_all | solution.py:23
  24.3 0.0 all-gather.5.cloned.1.call-start
  24.3 0.7 all-gather.5.cloned.1.call-update
  25.1 0.1 and_convert_fusion
  25.2 125.8 %all-gather.5.cloned.1.call-done = bf16[1,160,8192]{2,1,0:T(8,128)(2,1)} async-done(((bf16[1,160,512]{2,1,0:T(8,128)(2,1)}), bf16[1,160,8192]{2,1,0:T(8,128)(2,1)}) %all-gather.5.cloned.1.call-update) | async-done | bytes 2621456 | tf_op jit(solution)/shard_map/all_gather | solution.py:33
  151.0 4.5 fusion.11
  155.6 0.2 fusion.10
  155.9 2.7 dynamic_update_slice.3
  158.6 77.9 %all-reduce.1 = bf16[160,4,128]{2,1,0:T(4,128)(2,1)S(1)} all-reduce(f32[160,4,128]{2,1,0:T(4,128)S(1)} %dynamic_update_slice.3), channel_id=1, replica_groups=mesh['section'=32,'tp'=16] {'tp'}, use_global_device_ids=true, to_apply=%region_1.2 | all-reduce | flops 81920 | bytes 491520 | tf_op jit(solution)/shard_map/psum | solution.py:48
  236.5 1.0 fusion.33
  237.5 2.9 stack.3
  240.5 13.0 %all-to-all-start.1 = ((bf16[32,1,160,512]{3,2,1,0:T(8,128)(2,1)}), bf16[32,1,160,512]{3,2,1,0:T(8,128)(2,1)}, u32[]{:S(2)}, u32[]{:S(2)}) async-start(bf16[32,1,160,512]{3,2,1,0:T(8,128)(2,1)} %stack.3), calls=%async_computation.1 | async-start | bytes 10485760 | tf_op jit(solution)/shard_map/all_to_all | solution.py:57
  253.4 0.2 all-gather.7.cloned.1.call-start
  253.7 0.5 all-gather.7.cloned.1.call-update
  254.2 219.3 %all-gather.7.cloned.1.call-done = bf16[1,160,4096]{2,1,0:T(8,128)(2,1)} async-done(((bf16[1,160,256]{2,1,0:T(8,128)(2,1)}), bf16[1,160,4096]{2,1,0:T(8,128)(2,1)}) %all-gather.7.cloned.1.call-update) | async-done | bytes 1310736 | tf_op jit(solution)/shard_map/all_gather | solution.py:24
  473.5 1.6 copy.19
  475.1 3.7 convolution_convert_fusion
  478.8 5.3 copy.21
  484.2 5.6 copy.22
  489.8 1.5 fusion.38
  491.3 97.4 %psum.15 = f32[32,32]{1,0:T(8,128)S(1)} all-reduce(f32[32,32]{1,0:T(8,128)S(1)} %fusion.38), channel_id=1, replica_groups=mesh['section'=32,'tp'=16] {'tp'}, use_global_device_ids=true, to_apply=%region_2.3 | all-reduce | flops 1024 | bytes 8192 | tf_op jit(solution)/shard_map/psum | solution.py:77
  588.7 0.9 convolution_bitcast_fusion
  (18 shorter events, 0.1 us)
Async XLA Ops:
  7.2 229.3 %copy-start = (bf16[1,512,512]{2,1,0:T(8,128)(2,1)S(1)}, bf16[1,512,512]{2,1,0:T(8,128)(2,1)}, u32[]{:S(2)}) copy-start(bf16[1,512,512]{2,1,0:T(8,128)(2,1)} %param.9) | copy-start | bytes 1572868
  15.6 9.4 %copy-start.4 = (s32[160]{0:T(256)S(1)}, s32[160]{0:T(256)}, u32[]{:S(2)}) copy-start(s32[160]{0:T(256)} %param.12) | copy-start | bytes 1924
  15.6 221.9 %all-to-all-start = ((bf16[16,256,512]{2,1,0:T(8,128)(2,1)}), bf16[16,256,512]{2,1,0:T(8,128)(2,1)}, u32[]{:S(2)}, u32[]{:S(2)}) async-start(bf16[16,256,512]{2,1,0:T(8,128)(2,1)} %bitcast.65), calls=%async_computation | async-start | bytes 8388608 | tf_op jit(solution)/shard_map/all_to_all | solution.py:23
  24.3 126.7 %all-gather.5.cloned.1.call-start = ((), (), s32[]{:S(2)}) async-start(), calls=%async_computation.2 | async-start | bytes 2785280 | tf_op jit(solution)/shard_map/all_gather | solution.py:33
  25.2 130.4 %copy-start.3 = (bf16[1,2,160,160]{3,2,1,0:T(8,128)(2,1)S(1)}, bf16[1,2,160,160]{3,2,1,0:T(8,128)(2,1)}, u32[]{:S(2)}) copy-start(bf16[1,2,160,160]{3,2,1,0:T(8,128)(2,1)} %param.11) | copy-start | bytes 307204
  25.2 211.3 %copy-start.2 = (bf16[1,160,512]{2,1,0:T(8,128)(2,1)S(1)}, bf16[1,160,512]{2,1,0:T(8,128)(2,1)}, u32[]{:S(2)}) copy-start(bf16[1,160,512]{2,1,0:T(8,128)(2,1)} %param.7) | copy-start | bytes 491524
  240.5 243.7 %all-to-all-start.1 = ((bf16[32,1,160,512]{3,2,1,0:T(8,128)(2,1)}), bf16[32,1,160,512]{3,2,1,0:T(8,128)(2,1)}, u32[]{:S(2)}, u32[]{:S(2)}) async-start(bf16[32,1,160,512]{3,2,1,0:T(8,128)(2,1)} %stack.3), calls=%async_computation.1 | async-start | bytes 10485760 | tf_op jit(solution)/shard_map/all_to_all | solution.py:57
  253.4 220.1 %all-gather.7.cloned.1.call-start = ((), (), s32[]{:S(2)}) async-start(), calls=%async_computation.3 | async-start | bytes 1392640 | tf_op jit(solution)/shard_map/all_gather | solution.py:24
  484.2 5.6 copy-start.1
  489.8 98.9 %copy-start.5 = (s32[1,32]{1,0:T(1,128)S(1)}, s32[1,32]{1,0:T(1,128)}, u32[]{:S(2)}) copy-start(s32[1,32]{1,0:T(1,128)} %param.13) | copy-start | bytes 388
Sparse Core Ops, SparseCore 0:
  27.2 123.7 all-gather.4
  256.3 217.1 all-gather.6
